TPU v7x, 256 devices: a whole 4x4x8 slice. The times are simulated.
256 devices in a mesh: dp: 8 (over y, core), expert: 32 (over z, x).
Axes of the slice: x: 4, y: 4, z: 8, core: 2. Of those that a mesh axis runs over, the one named last changes fastest.
Arguments:
- tokens: bfloat16 [4096, 4096], P('expert', 'dp'), may hold values from -6 to 6
- expert_ids: int32 [4096, 8], P('expert'), may hold values from 0 to 63, all different within a row; in each aligned block of 128 rows (0 to 127, 128 to 255, ...) at most 24 rows name the same one
- route_weights: float32 [4096, 8], P('expert'), may hold values from 0.1 to 0.4
- gate_up_weight: bfloat16 [64, 4096, 1536], P('expert', 'dp'), may hold values from -0.09375 to 0.09375
- down_weight: bfloat16 [64, 768, 4096], P('expert', None, 'dp'), may hold values from -0.21875 to 0.21875
- out_grad: bfloat16 [4096, 4096], P('expert', 'dp'), may hold values from -6 to 6
Outputs:
- layer_out: bfloat16 [4096, 4096], P('expert', 'dp')
- token_grad: bfloat16 [4096, 4096], P('expert', 'dp')
- route_grad: float32 [4096, 8], P('expert')
- gate_up_grad: bfloat16 [64, 4096, 1536], P('expert', 'dp')
- down_grad: bfloat16 [64, 768, 4096], P('expert', None, 'dp')
Inputs may be any that keep to these rules, and one draw needn't show every extreme that they name: `expert_ids`: each row names 8 different experts. Among the 128 rows of one group no expert is named more than 24 times, and in every draw some group names some expert exactly 24 times.
All inputs are finite; a program needn't handle non-finite values.
Results may differ from a plain program's by a relative error of at most 0.029.
Values may be sent and summed in bfloat16 or wider, within the bound.
No kernel may reach another device: no remote copies, remote signals or barrier semaphores. Data moves between devices by JAX's collectives and lax.ppermute only.
A program may use at most 128 MiB of HBM per device.

v0:
```python
import jax
import jax.numpy as jnp
from jax import lax
from jax.sharding import PartitionSpec as P


def local(tokens, expert_ids, route_weights, gate_up_weight, down_weight, out_grad):
    tok_count, piece_width = tokens.shape
    top_count = expert_ids.shape[1]
    group_count = lax.axis_size("expert")
    local_count = gate_up_weight.shape[0]
    hidden_units = down_weight.shape[1]
    expert_total = local_count * group_count
    capacity = 3 * tok_count * top_count // (2 * expert_total)
    slot_count = expert_total * capacity
    rows_all = group_count * capacity
    route_count = tok_count * top_count
    block_shape = (local_count, group_count, capacity, piece_width)
    route_ids = expert_ids.reshape(-1)
    onehot = (route_ids[:, None] == jnp.arange(expert_total, dtype=jnp.int32)[None, :]).astype(
        jnp.bfloat16
    )
    order = jnp.arange(route_count, dtype=jnp.int32)
    lower = (order[None, :] < order[:, None]).astype(jnp.bfloat16)
    earlier = jnp.dot(lower, onehot, preferred_element_type=jnp.float32)
    slot_rank = jnp.sum(onehot.astype(jnp.float32) * earlier, axis=1).astype(jnp.int32)
    slot_index = (
        route_ids % local_count * rows_all + route_ids // local_count * capacity + slot_rank
    )
    route_hit = slot_index[:, None] == jnp.arange(slot_count, dtype=jnp.int32)[None, :]
    token_hit = jnp.any(route_hit.reshape(tok_count, top_count, slot_count), axis=1).astype(
        jnp.bfloat16
    )
    weight_flat = route_weights.reshape(-1)
    slot_weight = jnp.sum(jnp.where(route_hit, weight_flat[:, None], 0.0), axis=0)
    outbound = lax.dot_general(
        token_hit, tokens, (((0,), (0,)), ((), ())), preferred_element_type=jnp.float32
    ).astype(jnp.bfloat16)
    grad_outbound = (
        slot_weight[:, None]
        * lax.dot_general(
            token_hit, out_grad, (((0,), (0,)), ((), ())), preferred_element_type=jnp.float32
        )
    ).astype(jnp.bfloat16)
    both = jnp.stack([outbound, grad_outbound]).reshape((2,) + block_shape)
    both = lax.all_to_all(both, "expert", split_axis=2, concat_axis=2, tiled=True)
    arrived = both[0].reshape(local_count, rows_all, piece_width)
    grad_arrived = both[1].reshape(local_count, rows_all, piece_width)
    gate_up_part = jnp.einsum(
        "lrk,lkf->rlf", arrived, gate_up_weight, preferred_element_type=jnp.float32
    ).astype(jnp.bfloat16)
    hidden_grad_part = jnp.einsum(
        "lrk,lfk->rlf", grad_arrived, down_weight, preferred_element_type=jnp.float32
    ).astype(jnp.bfloat16)
    summed = lax.psum_scatter(
        jnp.concatenate([gate_up_part, hidden_grad_part], axis=2),
        "dp",
        scatter_dimension=0,
        tiled=True,
    ).astype(jnp.float32)
    gate_pre = summed[..., :hidden_units]
    up_pre = summed[..., hidden_units : 2 * hidden_units]
    hidden_grad = summed[..., 2 * hidden_units :]
    sigmoid_gate = jax.nn.sigmoid(gate_pre)
    activation = gate_pre * sigmoid_gate
    hidden_mine = (activation * up_pre).astype(jnp.bfloat16)
    gate_grad = hidden_grad * up_pre * sigmoid_gate * (1.0 + gate_pre * (1.0 - sigmoid_gate))
    up_grad = hidden_grad * activation
    preact_grad = jnp.concatenate([gate_grad, up_grad], axis=2).astype(jnp.bfloat16)
    hidden_all = lax.all_gather(hidden_mine, "dp", axis=0, tiled=True)
    preact_grad_all = lax.all_gather(preact_grad, "dp", axis=0, tiled=True)
    out_slice = jnp.einsum(
        "rlf,lfk->lrk", hidden_all, down_weight, preferred_element_type=jnp.float32
    ).astype(jnp.bfloat16)
    grad_routes = jnp.repeat(out_grad, top_count, axis=0).astype(jnp.float32)
    returned = lax.all_to_all(
        out_slice.reshape(block_shape), "expert", split_axis=1, concat_axis=1, tiled=True
    )
    route_pick = route_hit.astype(jnp.bfloat16)
    y_routes = jnp.dot(
        route_pick, returned.reshape(slot_count, piece_width), preferred_element_type=jnp.float32
    )
    layer_out = (
        (weight_flat[:, None] * y_routes)
        .reshape(tok_count, top_count, piece_width)
        .sum(axis=1)
        .astype(jnp.bfloat16)
    )
    partial_dot = jnp.sum(grad_routes * y_routes, axis=1).reshape(tok_count, top_count)
    route_grad = lax.psum(partial_dot, "dp")
    x_grad_slice = jnp.einsum(
        "rlf,lkf->lrk", preact_grad_all, gate_up_weight, preferred_element_type=jnp.float32
    ).astype(jnp.bfloat16)
    gate_up_grad = jnp.einsum(
        "lrk,rlf->lkf", arrived, preact_grad_all, preferred_element_type=jnp.float32
    ).astype(jnp.bfloat16)
    down_grad = jnp.einsum(
        "rlf,lrk->lfk", hidden_all, grad_arrived, preferred_element_type=jnp.float32
    ).astype(jnp.bfloat16)
    grad_back = lax.all_to_all(
        x_grad_slice.reshape(block_shape), "expert", split_axis=1, concat_axis=1, tiled=True
    )
    token_grad = jnp.dot(
        token_hit, grad_back.reshape(slot_count, piece_width), preferred_element_type=jnp.float32
    ).astype(jnp.bfloat16)
    return (layer_out, token_grad, route_grad, gate_up_grad, down_grad)


def solution(mesh):
    placed = (
        P("expert", "dp"),
        P("expert", None),
        P("expert", None),
        P("expert", "dp", None),
        P("expert", None, "dp"),
        P("expert", "dp"),
    )
    return jax.shard_map(
        local,
        mesh=mesh,
        in_specs=placed,
        out_specs=(
            P("expert", "dp"),
            P("expert", "dp"),
            P("expert", None),
            P("expert", "dp", None),
            P("expert", None, "dp"),
        ),
        check_vma=False,
    )
```

profile of v0, /device:TPU:4, one launch (start us, length us, event | category | flops | bytes accessed | tf_op | source)
XLA Modules:
  0.0 303.9 jit_solution(3204589052721626172)
XLA Ops:
  7.2 0.0 reduce-scatter.2.cloned.1.call-start
  7.2 0.9 copy.56
  8.2 0.1 reshape.107
  8.3 0.6 fusion.7
  8.9 0.8 copy.55
  9.7 0.1 mul.75
  9.8 0.1 convert_element_type.73
  9.9 0.1 fusion.13
  9.9 3.2 %fusion.1 = pred[128,1536]{1,0:T(8,128)(4,1)S(1)} fusion(s32[128,8]{1,0:T(8,128)S(1)} %fusion.13), kind=kLoop, calls=%fused_computation.5 | loop fusion | flops 2949120 | bytes 200704 | tf_op jit(solution)/shard_map/reduce_or | solution.py:31
  13.1 0.8 select_reduce_fusion
  13.9 1.5 convolution_convert_fusion.1
  15.5 0.6 fusion.4
  16.1 0.3 pad_maximum_fusion.1
  16.4 0.5 copy.74
  16.9 84.4 %all_to_all.15 = bf16[2,2,32,24,512]{4,3,1,0,2:T(8,128)(2,1)S(1)} all-to-all(bf16[2,2,32,24,512]{4,3,1,0,2:T(8,128)(2,1)S(1)} %copy.74), channel_id=1, replica_groups=mesh['dp'=8,'expert'=32] {'expert'}, dimensions={2} | all-to-all | bytes 6291456 | tf_op jit(solution)/shard_map/all_to_all | solution.py:46
  101.3 0.2 fusion.27
  101.5 0.1 copy.63
  101.7 0.1 copy.64
  101.8 4.2 %convert_bitcast_fusion = bf16[768,2,1536]{2,0,1:T(8,128)(2,1)} fusion(bf16[2,768,512]{2,1,0:T(8,128)(2,1)S(1)} %bitcast.40, bf16[2,512,1536]{2,1,0:T(8,128)(2,1)S(1)} %copy-done), kind=kOutput, calls=%fused_computation.6 | convolution fusion | flops 2418278400 | bytes 9437184 | tf_op jit(solution)/shard_map/lrk,lkf->rlf/dot_general | solution.py:49
  106.0 2.8 convert_bitcast_fusion.1
  108.9 6.4 %pad_maximum_fusion = bf16[768,2,2304]{2,0,1:T(8,128)(2,1)} fusion(bf16[768,2,768]{2,0,1:T(8,128)(2,1)} %convert_bitcast_fusion.1, bf16[768,2,1536]{2,0,1:T(8,128)(2,1)} %convert_bitcast_fusion), kind=kLoop, calls=%fused_computation | loop fusion | flops 14155776 | bytes 14155776 | tf_op jit(solution)/shard_map/concatenate | solution.py:56
  115.3 0.0 reduce-scatter.2.cloned.1.call-update
  115.3 0.0 all-gather.3.cloned.1.call-start
  115.4 45.8 %reduce-scatter.2.cloned.1.call-done = bf16[96,2,2304]{2,0,1:T(8,128)(2,1)} async-done(((bf16[768,2,2304]{2,0,1:T(8,128)(2,1)}), bf16[96,2,2304]{2,0,1:T(8,128)(2,1)}) %reduce-scatter.2.cloned.1.call-update) | async-done | bytes 884752 | tf_op jit(solution)/shard_map/reduce_scatter | solution.py:55
  161.2 1.3 convert_element_type.80
  162.5 1.2 multiply_convert_fusion.1
  163.6 0.0 all-gather.3.cloned.1.call-update
  163.7 0.0 all-gather.5.cloned.1.call-start
  163.7 1.9 pad_maximum_fusion.2
  165.6 26.0 %all-gather.3.cloned.1.call-done = bf16[768,2,768]{2,0,1:T(8,128)(2,1)} async-done(((bf16[96,2,768]{2,0,1:T(8,128)(2,1)}), bf16[768,2,768]{2,0,1:T(8,128)(2,1)}) %all-gather.3.cloned.1.call-update) | async-done | bytes 2359312 | tf_op jit(solution)/shard_map/all_gather | solution.py:70
  191.6 3.5 %convolution_convert_fusion.3 = bf16[2,768,512]{2,1,0:T(8,128)(2,1)S(1)} fusion(bf16[768,2,768]{2,0,1:T(8,128)(2,1)} %all-gather.3.cloned.1.call-done, bf16[2,768,512]{2,1,0:T(8,128)(2,1)} %param.10), kind=kOutput, calls=%fused_computation.20 | convolution fusion | flops 1208745984 | bytes 5505024 | tf_op jit(solution)/shard_map/rlf,lfk->lrk/dot_general | solution.py:72
  195.1 1.4 copy.66
  196.5 10.2 %all-to-all-start.1 = ((bf16[2,32,24,512]{3,2,0,1:T(8,128)(2,1)}), bf16[2,32,24,512]{3,2,0,1:T(8,128)(2,1)}, u32[]{:S(2)}, u32[]{:S(2)}) async-start(bf16[2,32,24,512]{3,2,0,1:T(8,128)(2,1)} %copy.66), calls=%async_computation.2 | async-start | bytes 3145728 | tf_op jit(solution)/shard_map/all_to_all | solution.py:76
  206.7 24.8 %all-gather.5.cloned.1.call-done = bf16[768,2,1536]{2,0,1:T(8,128)(2,1)} async-done(((bf16[96,2,1536]{2,0,1:T(8,128)(2,1)}), bf16[768,2,1536]{2,0,1:T(8,128)(2,1)}) %all-gather.5.cloned.1.call-update) | async-done | bytes 4718608 | tf_op jit(solution)/shard_map/all_gather | solution.py:71
  231.4 5.0 %convolution_convert_fusion.4 = bf16[2,768,512]{2,1,0:T(8,128)(2,1)S(1)} fusion(bf16[768,2,1536]{2,0,1:T(8,128)(2,1)} %all-gather.5.cloned.1.call-done, bf16[2,512,1536]{2,1,0:T(8,128)(2,1)S(1)} %copy-done), kind=kOutput, calls=%fused_computation.21 | convolution fusion | flops 2416705536 | bytes 9437184 | tf_op jit(solution)/shard_map/rlf,lkf->lrk/dot_general | solution.py:91
  236.4 1.4 copy.68
  237.8 8.6 %all-to-all-done.1 = bf16[2,32,24,512]{3,2,0,1:T(8,128)(2,1)} async-done(((bf16[2,32,24,512]{3,2,0,1:T(8,128)(2,1)}), bf16[2,32,24,512]{3,2,0,1:T(8,128)(2,1)}, u32[]{:S(2)}, u32[]{:S(2)}) %all-to-all-start.1) | async-done | bytes 1572896 | tf_op jit(solution)/shard_map/all_to_all | solution.py:76
  246.4 5.6 %all-to-all-start.2 = ((bf16[2,32,24,512]{3,2,0,1:T(8,128)(2,1)}), bf16[2,32,24,512]{3,2,0,1:T(8,128)(2,1)}, u32[]{:S(2)}, u32[]{:S(2)}) async-start(bf16[2,32,24,512]{3,2,0,1:T(8,128)(2,1)} %copy.68), calls=%async_computation.3 | async-start | bytes 3145728 | tf_op jit(solution)/shard_map/all_to_all | solution.py:100
  252.0 4.7 %convolution_convert_fusion.2 = bf16[2,768,512]{2,1,0:T(8,128)(2,1)} fusion(bf16[768,2,768]{2,0,1:T(8,128)(2,1)} %all-gather.3.cloned.1.call-done, bf16[2,768,512]{2,1,0:T(8,128)(2,1)} %bitcast.43), kind=kOutput, calls=%fused_computation.19 | convolution fusion | flops 1208745984 | bytes 5505024 | tf_op jit(solution)/shard_map/rlf,lrk->lfk/dot_general | solution.py:97
  256.7 1.5 copy.67
  258.3 2.9 bitcast_reduce_fusion
  261.2 0.3 fusion.5
  261.4 0.1 reshape.113
  261.5 25.5 %psum.7 = f32[128,8]{1,0:T(8,128)S(1)} all-reduce(f32[128,8]{1,0:T(8,128)S(1)} %reshape.113), channel_id=1, replica_groups=mesh['dp'=8,'expert'=32] {'dp'}, use_global_device_ids=true, to_apply=%region_6.7 | all-reduce | flops 1024 | bytes 8192 | tf_op jit(solution)/shard_map/psum | solution.py:90
  287.1 0.7 copy.71
  287.7 7.1 %convolution_convert_fusion = bf16[2,512,1536]{2,1,0:T(8,128)(2,1)} fusion(bf16[2,768,512]{2,1,0:T(8,128)(2,1)} %bitcast.41, bf16[768,2,1536]{2,0,1:T(8,128)(2,1)} %all-gather.5.cloned.1.call-done), kind=kOutput, calls=%fused_computation.9 | convolution fusion | flops 2417491968 | bytes 9437184 | tf_op jit(solution)/shard_map/lrk,rlf->lkf/dot_general | solution.py:94
  294.8 1.5 copy.69
  296.4 1.0 convolution_convert_fusion.5
  (15 shorter events, 0.1 us)
Async XLA Ops:
  7.2 94.6 %copy-start = (bf16[2,512,1536]{2,1,0:T(8,128)(2,1)S(1)}, bf16[2,512,1536]{2,1,0:T(8,128)(2,1)}, u32[]{:S(2)}) copy-start(bf16[2,512,1536]{2,1,0:T(8,128)(2,1)} %param.9) | copy-start | bytes 9437188
  7.2 154.0 %reduce-scatter.2.cloned.1.call-start = ((), (), s32[]{:S(2)}) async-start(), calls=%async_computation.4 | async-start | bytes 7962624 | tf_op jit(solution)/shard_map/reduce_scatter | solution.py:55
  8.3 7.2 %copy-start.3 = (bf16[128,512]{1,0:T(8,128)(2,1)S(1)}, bf16[128,512]{1,0:T(8,128)(2,1)}, u32[]{:S(2)}) copy-start(bf16[128,512]{1,0:T(8,128)(2,1)} %param.11) | copy-start | bytes 393220
  101.7 4.4 %copy-start.1 = (bf16[1,2,32,24,512]{4,3,2,1,0:T(8,128)(2,1)}, bf16[1,2,32,24,512]{4,3,2,1,0:T(8,128)(2,1)S(1)}, u32[]{:S(2)}) copy-start(bf16[1,2,32,24,512]{4,3,2,1,0:T(8,128)(2,1)S(1)} %copy.63) | copy-start | bytes 4718596
  101.8 4.2 %copy-start.2 = (bf16[1,2,32,24,512]{4,3,2,1,0:T(8,128)(2,1)}, bf16[1,2,32,24,512]{4,3,2,1,0:T(8,128)(2,1)S(1)}, u32[]{:S(2)}) copy-start(bf16[1,2,32,24,512]{4,3,2,1,0:T(8,128)(2,1)S(1)} %copy.64) | copy-start | bytes 4718596
  101.8 4.2 %copy-start.4 = (bf16[2,768,512]{2,1,0:T(8,128)(2,1)S(1)}, bf16[2,768,512]{2,1,0:T(8,128)(2,1)}, u32[]{:S(2)}) copy-start(bf16[2,768,512]{2,1,0:T(8,128)(2,1)} %param.10) | copy-start | bytes 4718596
  115.3 76.3 %all-gather.3.cloned.1.call-start = ((), (), s32[]{:S(2)}) async-start(), calls=%async_computation.5 | async-start | bytes 2654208 | tf_op jit(solution)/shard_map/all_gather | solution.py:70
  163.7 67.8 %all-gather.5.cloned.1.call-start = ((), (), s32[]{:S(2)}) async-start(), calls=%async_computation.6 | async-start | bytes 5308416 | tf_op jit(solution)/shard_map/all_gather | solution.py:71
  196.5 49.9 %all-to-all-start.1 = ((bf16[2,32,24,512]{3,2,0,1:T(8,128)(2,1)}), bf16[2,32,24,512]{3,2,0,1:T(8,128)(2,1)}, u32[]{:S(2)}, u32[]{:S(2)}) async-start(bf16[2,32,24,512]{3,2,0,1:T(8,128)(2,1)} %copy.66), calls=%async_computation.2 | async-start | bytes 3145728 | tf_op jit(solution)/shard_map/all_to_all | solution.py:76
  246.4 48.4 %all-to-all-start.2 = ((bf16[2,32,24,512]{3,2,0,1:T(8,128)(2,1)}), bf16[2,32,24,512]{3,2,0,1:T(8,128)(2,1)}, u32[]{:S(2)}, u32[]{:S(2)}) async-start(bf16[2,32,24,512]{3,2,0,1:T(8,128)(2,1)} %copy.68), calls=%async_computation.3 | async-start | bytes 3145728 | tf_op jit(solution)/shard_map/all_to_all | solution.py:100
Sparse Core Ops, SparseCore 0:
  115.4 45.7 reduce-scatter.1
  163.8 27.7 all-gather.2
  194.0 37.3 all-gather.4
where the time goes:
time: 304 us
  blocking collectives  110 us (36%)
  waiting for transfers between devices  105 us (35%)
  matrix products  34 us (11%)
  starting transfers between devices  15.9 us (5%)
  other arithmetic  15.4 us (5%)
  between operations  14 us (5%)
  local copies, waits for them, and re-layouts  9.53 us (3%)
    all_to_all x1, blocking collectives, local(): lax.all_to_all(both, 'expert', split_axis=2, concat_axis=2, tiled=True)  84.4 us
    reduce_scatter x1, waiting for transfers between devices, local(): lax.psum_scatter(jnp.concatenate([gate_up_part, hidden_grad_part], axis=2...  45.8 us
    all_gather x1, waiting for transfers between devices, local(): hidden_all = lax.all_gather(hidden_mine, 'dp', axis=0, tiled=True)  26 us
    psum x1, blocking collectives, local(): route_grad = lax.psum(partial_dot, 'dp')  25.5 us
    all_gather x1, waiting for transfers between devices, local(): preact_grad_all = lax.all_gather(preact_grad, 'dp', axis=0, tiled=True)  24.8 us
    all_to_all x1, starting transfers between devices, local(): lax.all_to_all(out_slice.reshape(block_shape), 'expert', split_axis=1, co...  10.2 us
    all_to_all x1, waiting for transfers between devices, local(): lax.all_to_all(out_slice.reshape(block_shape), 'expert', split_axis=1, co...  8.58 us
    dot_general x1, matrix products, local(): jnp.einsum('lrk,rlf->lkf', arrived, preact_grad_all, preferred_element_ty...  7.12 us
  transfers between devices with their start and end apart: 5, of which 4 were waited for; matrix products, arithmetic and copies ran while one was open for 10% of the time, Pallas kernels for 0%

commit v1 on v0

--- a/solution.py
+++ b/solution.py
@@ -67,7 +67,9 @@
     gate_grad = hidden_grad * up_pre * sigmoid_gate * (1.0 + gate_pre * (1.0 - sigmoid_gate))
     up_grad = hidden_grad * activation
     preact_grad = jnp.concatenate([gate_grad, up_grad], axis=2).astype(jnp.bfloat16)
-    hidden_all = lax.all_gather(hidden_mine, "dp", axis=0, tiled=True)
+    hidden_all = jnp.concatenate(
+        lax.all_to_all(jnp.stack([hidden_mine] * lax.axis_size("dp")), "dp", 0, 0), axis=0
+    )
     preact_grad_all = lax.all_gather(preact_grad, "dp", axis=0, tiled=True)
     out_slice = jnp.einsum(
         "rlf,lfk->lrk", hidden_all, down_weight, preferred_element_type=jnp.float32

time: 304 us -> 328 us (1.079)
  blocking collectives: 110 us -> 160 us
  waiting for transfers between devices: 105 us -> 77.3 us
    all_to_all x0 -> x1, blocking collectives: none -> 50.4 us  [local(): lax.all_to_all(jnp.stack([hidden_mine] * lax.axis_size('dp')), 'dp', 0, 0)]
    all_gather x1 -> x0, waiting for transfers between devices: 26 us -> none  [local(): hidden_all = lax.all_gather(hidden_mine, 'dp', axis=0, tiled=True)]
    all_gather x1, waiting for transfers between devices: 24.8 us -> 0.02 us  [local(): preact_grad_all = lax.all_gather(preact_grad, 'dp', axis=0, tiled=True)]
    all_to_all x1, waiting for transfers between devices: 8.58 us -> 31.5 us  [local(): lax.all_to_all(out_slice.reshape(block_shape), 'expert', split_axis=1, co...]
  transfers between devices with their start and end apart: 5 -> 4, of which waited for: 4 -> 2; matrix products, arithmetic and copies ran while one was open for 10% -> 8% of each run, Pallas kernels for 0% -> 0%
where the time goes in v1:
time: 328 us; the launch traced here: 327 us
  blocking collectives  160 us (49%)
  waiting for transfers between devices  77.3 us (24%)
  matrix products  31.9 us (10%)
  starting transfers between devices  16.4 us (5%)
  between operations  14.3 us (4%)
  other arithmetic  14.2 us (4%)
  local copies, waits for them, and re-layouts  12.8 us (4%)
    all_to_all x1, blocking collectives, local(): lax.all_to_all(both, 'expert', split_axis=2, concat_axis=2, tiled=True)  84.4 us
    all_to_all x1, blocking collectives, local(): lax.all_to_all(jnp.stack([hidden_mine] * lax.axis_size('dp')), 'dp', 0, 0)  50.4 us
    reduce_scatter x1, waiting for transfers between devices, local(): lax.psum_scatter(jnp.concatenate([gate_up_part, hidden_grad_part], axis=2...  45.8 us
    all_to_all x1, waiting for transfers between devices, local(): lax.all_to_all(out_slice.reshape(block_shape), 'expert', split_axis=1, co...  31.5 us
    psum x1, blocking collectives, local(): route_grad = lax.psum(partial_dot, 'dp')  25.5 us
    all_to_all x1, starting transfers between devices, local(): lax.all_to_all(out_slice.reshape(block_shape), 'expert', split_axis=1, co...  10.2 us
    dot_general x1, matrix products, local(): jnp.einsum('lrk,rlf->lkf', arrived, preact_grad_all, preferred_element_ty...  7.12 us
  transfers between devices with their start and end apart: 4, of which 2 were waited for; matrix products, arithmetic and copies ran while one was open for 8% of the time, Pallas kernels for 0%

profile of v1, /device:TPU:4, one launch (start us, length us, event | category | flops | bytes accessed | tf_op | source)
XLA Modules:
  0.0 327.2 jit_solution(7728983033630526296)
XLA Ops:
  7.2 0.0 reduce-scatter.2.cloned.1.call-start
  7.2 0.9 copy.62
  8.2 0.1 reshape.112
  8.3 0.6 fusion.7
  8.9 0.8 copy.61
  9.7 0.1 mul.75
  9.8 0.1 convert_element_type.73
  9.9 0.1 fusion.13
  10.0 3.2 fusion.1
  13.1 0.8 select_reduce_fusion
  13.9 1.5 convolution_convert_fusion.1
  15.5 0.6 fusion.4
  16.1 0.3 pad_maximum_fusion.1
  16.4 0.5 copy.83
  16.9 84.4 %all_to_all.20 = bf16[2,2,32,24,512]{4,3,1,0,2:T(8,128)(2,1)S(1)} all-to-all(bf16[2,2,32,24,512]{4,3,1,0,2:T(8,128)(2,1)S(1)} %copy.83), channel_id=1, replica_groups=mesh['dp'=8,'expert'=32] {'expert'}, dimensions={2} | all-to-all | bytes 6291456 | tf_op jit(solution)/shard_map/all_to_all | solution.py:46
  101.3 0.2 fusion.27
  101.5 0.1 copy.69
  101.7 0.1 copy.70
  101.8 4.2 %convert_bitcast_fusion = bf16[768,2,1536]{2,0,1:T(8,128)(2,1)} fusion(bf16[2,768,512]{2,1,0:T(8,128)(2,1)S(1)} %bitcast.43, bf16[2,512,1536]{2,1,0:T(8,128)(2,1)S(1)} %copy-done), kind=kOutput, calls=%fused_computation.6 | convolution fusion | flops 2418278400 | bytes 9437184 | tf_op jit(solution)/shard_map/lrk,lkf->rlf/dot_general | solution.py:49
  106.1 2.8 convert_bitcast_fusion.1
  108.9 6.4 %pad_maximum_fusion = bf16[768,2,2304]{2,0,1:T(8,128)(2,1)} fusion(bf16[768,2,768]{2,0,1:T(8,128)(2,1)} %convert_bitcast_fusion.1, bf16[768,2,1536]{2,0,1:T(8,128)(2,1)} %convert_bitcast_fusion), kind=kLoop, calls=%fused_computation | loop fusion | flops 14155776 | bytes 14155776 | tf_op jit(solution)/shard_map/concatenate | solution.py:56
  115.3 0.0 all-gather.2.cloned.1.call-start
  115.4 45.8 %reduce-scatter.2.cloned.1.call-done = bf16[96,2,2304]{2,0,1:T(8,128)(2,1)} async-done(((bf16[768,2,2304]{2,0,1:T(8,128)(2,1)}), bf16[96,2,2304]{2,0,1:T(8,128)(2,1)}) %reduce-scatter.2.cloned.1.call-update) | async-done | bytes 884752 | tf_op jit(solution)/shard_map/reduce_scatter | solution.py:55
  161.2 1.3 convert_element_type.80
  162.5 1.0 multiply_convert_fusion.1
  163.5 0.8 pad_maximum_fusion.2
  164.4 1.2 stack.11
  165.6 50.4 %all_to_all.21 = bf16[8,96,2,768]{3,1,2,0:T(8,128)(2,1)S(1)} all-to-all(bf16[8,96,2,768]{3,1,2,0:T(8,128)(2,1)S(1)} %stack.11), channel_id=1, replica_groups=mesh['dp'=8,'expert'=32] {'dp'}, dimensions={0} | all-to-all | bytes 4718592 | tf_op jit(solution)/shard_map/all_to_all | solution.py:71
  216.0 0.2 copy.72
  216.2 1.9 copy-done.6
  218.1 1.4 convolution_convert_fusion.3
  219.5 1.4 copy.73
  220.9 10.2 %all-to-all-start.2 = ((bf16[2,32,24,512]{3,2,0,1:T(8,128)(2,1)}), bf16[2,32,24,512]{3,2,0,1:T(8,128)(2,1)}, u32[]{:S(2)}, u32[]{:S(2)}) async-start(bf16[2,32,24,512]{3,2,0,1:T(8,128)(2,1)} %copy.73), calls=%async_computation.3 | async-start | bytes 3145728 | tf_op jit(solution)/shard_map/all_to_all | solution.py:78
  231.1 0.0 all-gather.2.cloned.1.call-done
  231.1 5.0 %convolution_convert_fusion.4 = bf16[2,768,512]{2,1,0:T(8,128)(2,1)S(1)} fusion(bf16[768,2,1536]{2,0,1:T(8,128)(2,1)} %all-gather.2.cloned.1.call-done, bf16[2,512,1536]{2,1,0:T(8,128)(2,1)S(1)} %copy-done), kind=kOutput, calls=%fused_computation.21 | convolution fusion | flops 2416705536 | bytes 9437184 | tf_op jit(solution)/shard_map/rlf,lkf->lrk/dot_general | solution.py:93
  236.1 1.4 copy.75
  237.4 31.5 %all-to-all-done.2 = bf16[2,32,24,512]{3,2,0,1:T(8,128)(2,1)} async-done(((bf16[2,32,24,512]{3,2,0,1:T(8,128)(2,1)}), bf16[2,32,24,512]{3,2,0,1:T(8,128)(2,1)}, u32[]{:S(2)}, u32[]{:S(2)}) %all-to-all-start.2) | async-done | bytes 1572896 | tf_op jit(solution)/shard_map/all_to_all | solution.py:78
  268.9 6.1 %all-to-all-start.3 = ((bf16[2,32,24,512]{3,2,0,1:T(8,128)(2,1)}), bf16[2,32,24,512]{3,2,0,1:T(8,128)(2,1)}, u32[]{:S(2)}, u32[]{:S(2)}) async-start(bf16[2,32,24,512]{3,2,0,1:T(8,128)(2,1)} %copy.75), calls=%async_computation.4 | async-start | bytes 3145728 | tf_op jit(solution)/shard_map/all_to_all | solution.py:102
  275.0 4.7 %convolution_convert_fusion.2 = bf16[2,768,512]{2,1,0:T(8,128)(2,1)} fusion(bf16[768,2,768]{2,0,1:T(8,128)(2,1)} %bitcast.42, bf16[2,768,512]{2,1,0:T(8,128)(2,1)} %bitcast.46), kind=kOutput, calls=%fused_computation.19 | convolution fusion | flops 1208745984 | bytes 5505024 | tf_op jit(solution)/shard_map/rlf,lrk->lfk/dot_general | solution.py:99
  279.7 1.5 copy.74
  281.3 2.9 bitcast_reduce_fusion
  284.2 0.3 fusion.5
  284.4 0.1 reshape.119
  284.5 25.5 %psum.7 = f32[128,8]{1,0:T(8,128)S(1)} all-reduce(f32[128,8]{1,0:T(8,128)S(1)} %reshape.119), channel_id=1, replica_groups=mesh['dp'=8,'expert'=32] {'dp'}, use_global_device_ids=true, to_apply=%region_6.7 | all-reduce | flops 1024 | bytes 8192 | tf_op jit(solution)/shard_map/psum | solution.py:92
  310.1 0.7 copy.79
  310.7 7.1 %convolution_convert_fusion = bf16[2,512,1536]{2,1,0:T(8,128)(2,1)} fusion(bf16[2,768,512]{2,1,0:T(8,128)(2,1)} %bitcast.44, bf16[768,2,1536]{2,0,1:T(8,128)(2,1)} %all-gather.2.cloned.1.call-done), kind=kOutput, calls=%fused_computation.9 | convolution fusion | flops 2417491968 | bytes 9437184 | tf_op jit(solution)/shard_map/lrk,rlf->lkf/dot_general | solution.py:96
  317.8 1.5 copy.76
  319.4 1.0 convolution_convert_fusion.5
  (19 shorter events, 0.1 us)
Async XLA Ops:
  7.2 94.7 %copy-start = (bf16[2,512,1536]{2,1,0:T(8,128)(2,1)S(1)}, bf16[2,512,1536]{2,1,0:T(8,128)(2,1)}, u32[]{:S(2)}) copy-start(bf16[2,512,1536]{2,1,0:T(8,128)(2,1)} %param.9) | copy-start | bytes 9437188
  7.2 8.3 %copy-start.4 = (bf16[128,512]{1,0:T(8,128)(2,1)S(1)}, bf16[128,512]{1,0:T(8,128)(2,1)}, u32[]{:S(2)}) copy-start(bf16[128,512]{1,0:T(8,128)(2,1)} %param.11) | copy-start | bytes 393220
  7.2 154.0 %reduce-scatter.2.cloned.1.call-start = ((), (), s32[]{:S(2)}) async-start(), calls=%async_computation.5 | async-start | bytes 7962624 | tf_op jit(solution)/shard_map/reduce_scatter | solution.py:55
  101.7 4.4 %copy-start.2 = (bf16[1,2,32,24,512]{4,3,2,1,0:T(8,128)(2,1)}, bf16[1,2,32,24,512]{4,3,2,1,0:T(8,128)(2,1)S(1)}, u32[]{:S(2)}) copy-start(bf16[1,2,32,24,512]{4,3,2,1,0:T(8,128)(2,1)S(1)} %copy.69) | copy-start | bytes 4718596
  101.8 4.2 %copy-start.3 = (bf16[1,2,32,24,512]{4,3,2,1,0:T(8,128)(2,1)}, bf16[1,2,32,24,512]{4,3,2,1,0:T(8,128)(2,1)S(1)}, u32[]{:S(2)}) copy-start(bf16[1,2,32,24,512]{4,3,2,1,0:T(8,128)(2,1)S(1)} %copy.70) | copy-start | bytes 4718596
  101.8 4.2 %copy-start.5 = (bf16[2,768,512]{2,1,0:T(8,128)(2,1)S(1)}, bf16[2,768,512]{2,1,0:T(8,128)(2,1)}, u32[]{:S(2)}) copy-start(bf16[2,768,512]{2,1,0:T(8,128)(2,1)} %param.10) | copy-start | bytes 4718596
  115.3 115.7 %all-gather.2.cloned.1.call-start = ((), (), s32[]{:S(2)}) async-start(), calls=%async_computation.6 | async-start | bytes 5308416 | tf_op jit(solution)/shard_map/all_gather | solution.py:73
  216.0 2.1 copy-start.6
  216.2 3.3 %copy-start.1 = (bf16[8,96,2,768]{3,1,0,2:T(8,128)(2,1)}, bf16[8,96,2,768]{3,1,0,2:T(8,128)(2,1)S(1)}, u32[]{:S(2)}) copy-start(bf16[8,96,2,768]{3,1,0,2:T(8,128)(2,1)S(1)} %copy.72) | copy-start | bytes 7077892
  220.9 48.0 %all-to-all-start.2 = ((bf16[2,32,24,512]{3,2,0,1:T(8,128)(2,1)}), bf16[2,32,24,512]{3,2,0,1:T(8,128)(2,1)}, u32[]{:S(2)}, u32[]{:S(2)}) async-start(bf16[2,32,24,512]{3,2,0,1:T(8,128)(2,1)} %copy.73), calls=%async_computation.3 | async-start | bytes 3145728 | tf_op jit(solution)/shard_map/all_to_all | solution.py:78
  268.9 49.0 %all-to-all-start.3 = ((bf16[2,32,24,512]{3,2,0,1:T(8,128)(2,1)}), bf16[2,32,24,512]{3,2,0,1:T(8,128)(2,1)}, u32[]{:S(2)}, u32[]{:S(2)}) async-start(bf16[2,32,24,512]{3,2,0,1:T(8,128)(2,1)} %copy.75), calls=%async_computation.4 | async-start | bytes 3145728 | tf_op jit(solution)/shard_map/all_to_all | solution.py:102
Sparse Core Ops, SparseCore 0:
  115.5 45.7 reduce-scatter.1
  164.5 53.7 all-gather.1
